TPU v7x, 32 devices: a whole 2x2x4 slice. The times are simulated.
32 devices in a mesh: ctx: 16 (over z, y, core), head: 2 (over x).
Axes of the slice: x: 2, y: 2, z: 4, core: 2. Of those that a mesh axis runs over, the one named last changes fastest.
Arguments:
- queries: bfloat16 [2048, 1536], P('ctx', 'head'), may hold values from -45 to 45
- key_rows: bfloat16 [2048, 256], P('ctx', 'head'), may hold values from -5 to 5
- value_rows: bfloat16 [2048, 256], P('ctx', 'head'), may hold values from -18 to 18
- cotangent: bfloat16 [2048, 1536], P('ctx', 'head'), may hold values from -6 to 6
- trace_ids: int32 [2048], P('ctx'), may hold values from 0 to 15, never falling along the last dimension, each value on 1 to 512 neighbouring positions
- correct: int32 [16], replicated, may hold values from 0 to 16, as said below
- group_size: int32 [16], replicated, may hold values from 4 to 16
Outputs:
- log_totals: float32 [2048, 12], P('ctx', 'head')
- grad_queries: float32 [2048, 1536], P('ctx', 'head')
- grad_keys: bfloat16 [2048, 256], P('ctx', 'head')
- grad_values: bfloat16 [2048, 256], P('ctx', 'head')
Inputs may be any that keep to these rules, and one draw needn't show every extreme that they name: correct[g] is at most group_size[g].
All inputs are finite; a program needn't handle non-finite values.
Results may differ from a plain program's by a relative error of at most 0.0054.
Values may be sent and summed in bfloat16 or wider, within the bound.
No kernel may reach another device: no remote copies, remote signals or barrier semaphores. Data moves between devices by JAX's collectives and lax.ppermute only.
A program may use at most 64 MiB of HBM per device.

v0:
```python
import math
import jax
import jax.numpy as jnp
from jax import lax
from jax.sharding import PartitionSpec as P

PASSK = 4


def pass_rate(correct, group_size):
    counts = group_size.astype(jnp.float32)
    hit_counts = correct.astype(jnp.float32)
    product = jnp.ones_like(counts)
    for offset in range(PASSK):
        product = product * (counts - hit_counts - offset) / (counts - offset)
    return 1.0 - product


def body(queries, key_rows, value_rows, cotangent, trace_ids, correct, group_size):
    tok_rows = queries.shape[0]
    half_rows = tok_rows // 2
    row_width = queries.shape[1]
    head_dim = key_rows.shape[1]
    head_count = row_width // head_dim
    ctx_count = lax.axis_size("ctx")
    my_index = lax.axis_index("ctx")
    length = tok_rows * ctx_count
    score_scale = 1.0 / math.sqrt(head_dim)
    pass_rates = pass_rate(correct, group_size)
    traces = jnp.arange(pass_rates.shape[0], dtype=jnp.int32)
    weights = jnp.sum(
        jnp.where(trace_ids[:, None] == traces[None, :], pass_rates[None, :], 0.0), axis=1
    )
    out_grads = (weights[:, None] * cotangent.astype(jnp.float32)).astype(jnp.bfloat16)
    first_base = my_index * tok_rows
    second_base = first_base + half_rows
    local_pos = jnp.arange(half_rows, dtype=jnp.int32)
    positions = jnp.concatenate([first_base + local_pos, second_base + local_pos], 0)
    last_first = first_base + half_rows - 1
    last_second = second_base + half_rows - 1
    query_all = queries.reshape(tok_rows, head_count, head_dim)
    grad_all = out_grads.reshape(tok_rows, head_count, head_dim)

    def run_block(running, key_block, value_block, key_start, block_fn):
        need_first = (key_start <= last_first).astype(jnp.int32)
        need_second = (key_start <= last_second).astype(jnp.int32)
        branch_index = need_first + 2 * need_second

        def skip_block(values_in):
            return values_in

        def first_only(values_in):
            return block_fn((0, half_rows), values_in, key_block, value_block, key_start)

        def second_only(values_in):
            return block_fn((half_rows, tok_rows), values_in, key_block, value_block, key_start)

        def both_halves(values_in):
            return block_fn((0, tok_rows), values_in, key_block, value_block, key_start)

        return lax.switch(branch_index, [skip_block, first_only, second_only, both_halves], running)

    def forward_block(row_span, running, key_block, value_block, key_start):
        row_begin, row_end = row_span
        row_peak, row_total, weighted = running
        query_part = query_all[row_begin:row_end]
        grad_part = grad_all[row_begin:row_end]
        query_pos = positions[row_begin:row_end]
        scores = (
            jnp.einsum("tqd,kd->tqk", query_part, key_block, preferred_element_type=jnp.float32)
            * score_scale
        )
        key_pos = key_start + jnp.arange(key_block.shape[0], dtype=jnp.int32)
        visible = key_pos[None, None, :] <= query_pos[:, None, None]
        block_peak = jnp.max(jnp.where(visible, scores, -1e30), axis=2)
        old_peak = row_peak[row_begin:row_end]
        new_peak = jnp.maximum(old_peak, block_peak)
        exp_terms = jnp.where(visible, jnp.exp(scores - new_peak[:, :, None]), 0.0)
        grad_probs = jnp.einsum(
            "tqd,kd->tqk", grad_part, value_block, preferred_element_type=jnp.float32
        )
        shrink = jnp.exp(old_peak - new_peak)
        new_total = row_total[row_begin:row_end] * shrink + jnp.sum(exp_terms, axis=2)
        new_weighted = weighted[row_begin:row_end] * shrink + jnp.sum(
            exp_terms * grad_probs, axis=2
        )
        return (
            row_peak.at[row_begin:row_end].set(new_peak),
            row_total.at[row_begin:row_end].set(new_total),
            weighted.at[row_begin:row_end].set(new_weighted),
        )

    row_peak = jnp.full((tok_rows, head_count), -1e30, jnp.float32)
    row_total = jnp.zeros((tok_rows, head_count), jnp.float32)
    weighted = jnp.zeros((tok_rows, head_count), jnp.float32)
    key_piece = lax.all_gather(key_rows, "ctx", axis=0, tiled=True)
    value_piece = lax.all_gather(value_rows, "ctx", axis=0, tiled=True)
    piece_rows = key_piece.shape[0]
    block_rows = math.gcd(piece_rows, 512)

    def forward_step(step_index, statistics):
        offset = step_index * block_rows
        key_block = lax.dynamic_slice_in_dim(key_piece, offset, block_rows, 0)
        value_block = lax.dynamic_slice_in_dim(value_piece, offset, block_rows, 0)
        return run_block(statistics, key_block, value_block, offset, forward_block)

    statistics = lax.fori_loop(
        0, piece_rows // block_rows, forward_step, (row_peak, row_total, weighted)
    )
    folded = statistics + (key_piece, value_piece)
    row_peak, row_total, weighted, key_store, value_store = folded
    log_totals = row_peak + jnp.log(row_total)
    delta_rows = weighted / row_total

    def backward_block(row_span, running, key_block, value_block, key_start):
        row_begin, row_end = row_span
        grad_query, zero_block = running
        query_part = query_all[row_begin:row_end]
        grad_part = grad_all[row_begin:row_end]
        query_pos = positions[row_begin:row_end]
        scores = (
            jnp.einsum("tqd,kd->tqk", query_part, key_block, preferred_element_type=jnp.float32)
            * score_scale
        )
        key_pos = key_start + jnp.arange(key_block.shape[0], dtype=jnp.int32)
        visible = key_pos[None, None, :] <= query_pos[:, None, None]
        probabilities = jnp.where(
            visible, jnp.exp(scores - log_totals[row_begin:row_end][:, :, None]), 0.0
        )
        prob_bf16 = probabilities.astype(jnp.bfloat16)
        grad_probs = jnp.einsum(
            "tqd,kd->tqk", grad_part, value_block, preferred_element_type=jnp.float32
        )
        grad_scores = (
            probabilities * (grad_probs - delta_rows[row_begin:row_end][:, :, None])
        ).astype(jnp.bfloat16)
        query_add = (
            jnp.einsum("tqk,kd->tqd", grad_scores, key_block, preferred_element_type=jnp.float32)
            * score_scale
        )
        key_add = (
            jnp.einsum("tqk,tqd->kd", grad_scores, query_part, preferred_element_type=jnp.float32)
            * score_scale
        )
        value_add = jnp.einsum(
            "tqk,tqd->kd", prob_bf16, grad_part, preferred_element_type=jnp.float32
        )
        return (
            grad_query.at[row_begin:row_end].add(query_add),
            jnp.concatenate([key_add, value_add], 1),
        )

    query_zero = jnp.zeros((tok_rows, head_count, head_dim), jnp.float32)
    key_block_rows = math.gcd(length, 512)

    def backward_step(step_index, running):
        grad_query, partial_sums = running
        key_start = step_index * key_block_rows
        key_block = lax.dynamic_slice_in_dim(key_store, key_start, key_block_rows, 0)
        value_block = lax.dynamic_slice_in_dim(value_store, key_start, key_block_rows, 0)
        zero_block = jnp.zeros((key_block_rows, 2 * head_dim), jnp.float32)
        grad_query, block_sums = run_block(
            (grad_query, zero_block), key_block, value_block, key_start, backward_block
        )
        partial_sums = lax.dynamic_update_slice_in_dim(partial_sums, block_sums, key_start, 0)
        return (grad_query, partial_sums)

    grad_query, partial_sums = lax.fori_loop(
        0,
        length // key_block_rows,
        backward_step,
        (query_zero, jnp.zeros((length, 2 * head_dim), jnp.float32)),
    )
    reduced = jnp.sum(
        lax.all_to_all(
            partial_sums.reshape(ctx_count, tok_rows, 2 * head_dim),
            "ctx",
            split_axis=0,
            concat_axis=0,
            tiled=True,
        ),
        axis=0,
    )
    grad_keys = reduced[:, :head_dim].astype(jnp.bfloat16)
    grad_values = reduced[:, head_dim:].astype(jnp.bfloat16)
    query_grads = grad_query.reshape(tok_rows, row_width)
    return (log_totals, query_grads, grad_keys, grad_values)


def solution(mesh):
    return jax.shard_map(
        body,
        mesh=mesh,
        in_specs=(
            P("ctx", "head"),
            P("ctx", "head"),
            P("ctx", "head"),
            P("ctx", "head"),
            P("ctx"),
            P(),
            P(),
        ),
        out_specs=(P("ctx", "head"), P("ctx", "head"), P("ctx", "head"), P("ctx", "head")),
        check_vma=False,
    )
```

profile of v0, /device:TPU:13, one launch (start us, length us, event | category | flops | bytes accessed | tf_op | source)
XLA Modules:
  0.0 124.0 jit_solution(4631487437105801853)
XLA Ops:
  0.6 0.0 copy-start.1
  0.6 0.0 copy-start.2
  0.7 0.7 fusion.61
  1.4 0.7 select_reduce_fusion.3
  2.1 1.0 multiply_convert_fusion.1
  3.1 0.2 copy.73
  3.3 0.2 copy.75
  3.5 1.1 copy.72
  4.6 0.2 copy.74
  4.8 0.0 copy-done.1
  4.8 17.1 %all_gather.6 = bf16[2048,128]{1,0:T(8,128)(2,1)S(1)} all-gather(bf16[128,128]{1,0:T(8,128)(2,1)S(1)} %copy-done.1), channel_id=1, replica_groups=mesh['ctx'=16,'head'=2] {'ctx'}, dimensions={0}, use_global_device_ids=true | all-gather | bytes 557056 | tf_op jit(solution)/shard_map/all_gather | solution.py:96
  21.9 0.0 copy-done.2
  21.9 22.8 %all_gather.7 = bf16[2048,128]{1,0:T(8,128)(2,1)S(1)} all-gather(bf16[128,128]{1,0:T(8,128)(2,1)S(1)} %copy-done.2), channel_id=1, replica_groups=mesh['ctx'=16,'head'=2] {'ctx'}, dimensions={0}, use_global_device_ids=true | all-gather | bytes 557056 | tf_op jit(solution)/shard_map/all_gather | solution.py:97
  44.7 0.1 pad_add_fusion
  44.8 3.9 %while.53 = (s32[]{:T(128)}, f32[128,6]{0,1:T(8,128)S(1)}, f32[128,6]{0,1:T(8,128)S(1)}, f32[128,6]{0,1:T(8,128)S(1)}, s32[]{:T(128)}, /*index=5*/s32[]{:T(128)}...) while((s32[]{:T(128)}, f32[128,6]{0,1:T(8,128)S(1)}, ...), condition=%wide.region_15.0_spmd.clone, body=%wide.region_1.15_spmd.clone.sunk | while | flops 205327120 | bytes 6221379 | solution.py:107
  44.8 1.7 %conditional.6 = ((f32[128,6]{0,1:T(8,128)S(1)}, f32[128,6]{0,1:T(8,128)S(1)}, f32[128,6]{0,1:T(8,128)S(1)})) conditional(s32[]{:T(128)} %clamp.18, (f32[128,6]{0,1:T(8,128)S(1)}, f32[128,6]{0,1:T(8,128)S(1)}, f32[128,6]{0,1:T(8,128)S(1)}) %tuple.202, (f32[128,6]{0,1:T(8,128)S(1)}, s32[]{:T(128)}, s32[]{:T(128)}, ...), branch_computations={%region_2.2_spmd, %region_3.6_spmd, %region_7.10_spmd, %region_11.... | conditional | flops 205327104 | bytes 5696036 | solution.py:61
  44.9 0.1 broadcast_compare_fusion.2
  45.0 0.5 select_reduce_fusion.2
  45.4 0.6 multiply_reduce_fusion
  46.0 0.5 fusion.20
  46.6 1.7 %conditional.6 = ((f32[128,6]{0,1:T(8,128)S(1)}, f32[128,6]{0,1:T(8,128)S(1)}, f32[128,6]{0,1:T(8,128)S(1)})) conditional(s32[]{:T(128)} %clamp.18, (f32[128,6]{0,1:T(8,128)S(1)}, f32[128,6]{0,1:T(8,128)S(1)}, f32[128,6]{0,1:T(8,128)S(1)}) %tuple.202, (f32[128,6]{0,1:T(8,128)S(1)}, s32[]{:T(128)}, s32[]{:T(128)}, ...), branch_computations={%region_2.2_spmd, %region_3.6_spmd, %region_7.10_spmd, %region_11.... | conditional | flops 205327104 | bytes 5696036 | solution.py:61
  46.7 0.1 broadcast_compare_fusion.2
  46.8 0.5 select_reduce_fusion.2
  47.3 0.6 multiply_reduce_fusion
  47.8 0.5 fusion.20
  48.7 1.5 %broadcast_in_dim.124.clone = f32[2048,256]{1,0:T(8,128)} broadcast(f32[]{:T(128)} %constant.488.clone.1), dimensions={} | broadcast | bytes 2097156 | tf_op jit(solution)/shard_map/broadcast_in_dim | solution.py:172
  50.2 8.7 %while.54 = (s32[]{:T(128)}, f32[128,6,128]{2,0,1:T(8,128)S(1)}, f32[2048,256]{1,0:T(8,128)}, s32[]{:T(128)}, s32[]{:T(128)}, /*index=5*/bf16[2048,128]{1,0:T(8,...) while((s32[]{:T(128)}, f32[128,6,128]{2,0,1:T(8,128)S(1)}, ...), condition=%wide.region_21.22_spmd.clone, body=%wide.region_16.21_spmd.clone.sunk | while | flops 506528256 | bytes 13381159 | solution.py:168
  50.2 2.1 %conditional.7 = (f32[128,6,128]{2,0,1:T(8,128)S(1)}, f32[512,256]{0,1:T(8,128)S(1)}) conditional(s32[]{:T(128)} %clamp.19, f32[128,6,128]{2,0,1:T(8,128)S(1)} %get-tuple-element.1421, (f32[128,6,128]{2,0,1:T(8,128)S(1)}, s32[]{:T(128)}, s32[]{:T(128)}, bf16[128,6,128]{0,2,1:T(8,128)(2,1)S(1)}, ...), branch_computations={%region_17.17_spmd, %region_18.18_spmd, %region_19.19_spmd, %regio... | conditional | flops 506528256 | bytes 10758676 | solution.py:61
  50.2 0.1 broadcast_compare_fusion.5
  50.4 0.5 exponential_select_fusion.3
  50.9 0.3 convolution_bitcast_fusion.4
  51.2 0.4 multiply_convert_fusion
  51.6 0.3 fusion.56
  51.9 0.4 fusion.55
  52.3 0.2 copy.91
  52.5 0.8 constant_dynamic-update-slice_fusion.2
  53.4 2.1 %conditional.7 = (f32[128,6,128]{2,0,1:T(8,128)S(1)}, f32[512,256]{0,1:T(8,128)S(1)}) conditional(s32[]{:T(128)} %clamp.19, f32[128,6,128]{2,0,1:T(8,128)S(1)} %get-tuple-element.1421, (f32[128,6,128]{2,0,1:T(8,128)S(1)}, s32[]{:T(128)}, s32[]{:T(128)}, bf16[128,6,128]{0,2,1:T(8,128)(2,1)S(1)}, ...), branch_computations={%region_17.17_spmd, %region_18.18_spmd, %region_19.19_spmd, %regio... | conditional | flops 506528256 | bytes 10758676 | solution.py:61
  53.4 0.1 broadcast_compare_fusion.5
  53.5 0.5 exponential_select_fusion.3
  54.1 0.3 convolution_bitcast_fusion.4
  54.3 0.4 multiply_convert_fusion
  54.8 0.3 fusion.56
  55.0 0.4 fusion.55
  55.5 0.2 copy.91
  55.7 0.9 constant_dynamic-update-slice_fusion.2
  56.6 0.1 conditional.7
  56.6 0.1 broadcast.400
  56.7 0.2 copy.91
  56.9 0.9 constant_dynamic-update-slice_fusion.2
  57.7 0.1 conditional.7
  57.8 0.1 broadcast.400
  57.8 0.2 copy.91
  58.1 0.9 constant_dynamic-update-slice_fusion.2
  58.9 0.0 copy-start
  58.9 2.9 %copy.78 = f32[16,128,256]{1,2,0:T(8,128)} copy(f32[16,128,256]{2,1,0:T(8,128)} %bitcast.88) | data formatting | bytes 4194304 | tf_op jit(solution)/shard_map/reshape | solution.py:176
  61.8 0.0 copy-done
  61.8 13.2 %all-to-all-start = ((f32[16,128,256]{1,2,0:T(8,128)}), f32[16,128,256]{1,2,0:T(8,128)S(1)}, u32[]{:S(2)}, u32[]{:S(2)}) async-start(f32[16,128,256]{1,2,0:T(8,128)} %copy.78), calls=%async_computation | async-start | bytes 4194304 | tf_op jit(solution)/shard_map/all_to_all | solution.py:175
  75.0 0.2 copy.76
  75.2 0.9 copy.80
  76.1 46.3 %all-to-all-done = f32[16,128,256]{1,2,0:T(8,128)S(1)} async-done(((f32[16,128,256]{1,2,0:T(8,128)}), f32[16,128,256]{1,2,0:T(8,128)S(1)}, u32[]{:S(2)}, u32[]{:S(2)}) %all-to-all-start) | async-done | bytes 2097184 | tf_op jit(solution)/shard_map/all_to_all | solution.py:175
  122.4 0.1 reduce_sum.73
  122.5 0.7 copy.82
  123.2 0.7 copy.81
  (45 shorter events, 0.5 us)
Async XLA Ops:
  0.6 4.1 %copy-start.1 = (bf16[128,128]{1,0:T(8,128)(2,1)S(1)}, bf16[128,128]{1,0:T(8,128)(2,1)}, u32[]{:S(2)}) copy-start(bf16[128,128]{1,0:T(8,128)(2,1)} %param.52) | copy-start | bytes 98308
  0.6 21.2 %copy-start.2 = (bf16[128,128]{1,0:T(8,128)(2,1)S(1)}, bf16[128,128]{1,0:T(8,128)(2,1)}, u32[]{:S(2)}) copy-start(bf16[128,128]{1,0:T(8,128)(2,1)} %param.53) | copy-start | bytes 98308
  58.9 2.9 %copy-start = (f32[128,6]{0,1:T(8,128)}, f32[128,6]{0,1:T(8,128)S(1)}, u32[]{:S(2)}) copy-start(f32[128,6]{0,1:T(8,128)S(1)} %get-tuple-element.1469) | copy-start | bytes 9220
  61.8 60.6 %all-to-all-start = ((f32[16,128,256]{1,2,0:T(8,128)}), f32[16,128,256]{1,2,0:T(8,128)S(1)}, u32[]{:S(2)}, u32[]{:S(2)}) async-start(f32[16,128,256]{1,2,0:T(8,128)} %copy.78), calls=%async_computation | async-start | bytes 4194304 | tf_op jit(solution)/shard_map/all_to_all | solution.py:175
where the time goes:
time: 124 us
  waiting for transfers between devices  46.3 us (37%)
  blocking collectives  39.9 us (32%)
  starting transfers between devices  13.2 us (11%)
  local copies, waits for them, and re-layouts  13.1 us (11%)
  matrix products  5.79 us (5%)
  other arithmetic  4.14 us (3%)
    all_to_all x1, waiting for transfers between devices, body(): lax.all_to_all(partial_sums.reshape(ctx_count, tok_rows, 2 * head_dim), '...  46.3 us
    all_gather x1, blocking collectives, body(): value_piece = lax.all_gather(value_rows, 'ctx', axis=0, tiled=True)  22.8 us
    all_gather x1, blocking collectives, body(): key_piece = lax.all_gather(key_rows, 'ctx', axis=0, tiled=True)  17.1 us
    all_to_all x1, starting transfers between devices, body(): lax.all_to_all(partial_sums.reshape(ctx_count, tok_rows, 2 * head_dim), '...  13.2 us
    dynamic_update_slice x8, local copies, waits for them, and re-layouts, backward_step(): lax.dynamic_update_slice_in_dim(partial_sums, block_sums, key_start, 0)  4.17 us
    unnamed x12, local copies, waits for them, and re-layouts  3.83 us
    reshape x1, local copies, waits for them, and re-layouts, body(): partial_sums.reshape(ctx_count, tok_rows, 2 * head_dim)  2.89 us
  transfers between devices with their start and end apart: 1, of which 1 were waited for; matrix products, arithmetic and copies ran while one was open for 1% of the time, Pallas kernels for 0%

commit v1 on v0

--- a/solution.py
+++ b/solution.py
@@ -93,8 +93,11 @@
     row_peak = jnp.full((tok_rows, head_count), -1e30, jnp.float32)
     row_total = jnp.zeros((tok_rows, head_count), jnp.float32)
     weighted = jnp.zeros((tok_rows, head_count), jnp.float32)
-    key_piece = lax.all_gather(key_rows, "ctx", axis=0, tiled=True)
-    value_piece = lax.all_gather(value_rows, "ctx", axis=0, tiled=True)
+    key_piece, value_piece = jnp.split(
+        lax.all_gather(jnp.concatenate([key_rows, value_rows], axis=1), "ctx", axis=0, tiled=True),
+        [key_rows.shape[1]],
+        1,
+    )
     piece_rows = key_piece.shape[0]
     block_rows = math.gcd(piece_rows, 512)
 

time: 124 us -> 136 us (1.097)
  blocking collectives: 39.9 us -> 0 us
  waiting for transfers between devices: 46.3 us -> 82.5 us
  between operations: 0.74 us -> 14.1 us
  other arithmetic: 4.14 us -> 5.55 us
    all_gather x2 -> x0, blocking collectives: 39.9 us -> none  [the longest x1 22.8 us: body(): value_piece = lax.all_gather(value_rows, 'ctx', axis=0, tiled=True)]
    all_gather x0 -> x1, waiting for transfers between devices: none -> 36.2 us  [body(): lax.all_gather(jnp.concatenate([key_rows, value_rows], axis=1), 'ctx', ax...]
    concatenate x0 -> x1, other arithmetic: none -> 1.41 us  [body(): jnp.concatenate([key_rows, value_rows], axis=1)]
    unnamed x12 -> x8, local copies, waits for them, and re-layouts: 3.83 us -> 3.82 us
  transfers between devices with their start and end apart: 1 -> 2, of which waited for: 1 -> 2; matrix products, arithmetic and copies ran while one was open for 1% -> 4% of each run, Pallas kernels for 0% -> 0%
where the time goes in v1:
time: 136 us
  waiting for transfers between devices  82.5 us (61%)
  local copies, waits for them, and re-layouts  14.3 us (11%)
  between operations  14.1 us (10%)
  starting transfers between devices  12.6 us (9%)
  matrix products  5.79 us (4%)
  other arithmetic  5.55 us (4%)
    all_to_all x1, waiting for transfers between devices, body(): lax.all_to_all(partial_sums.reshape(ctx_count, tok_rows, 2 * head_dim), '...  46.3 us
    all_gather x1, waiting for transfers between devices, body(): lax.all_gather(jnp.concatenate([key_rows, value_rows], axis=1), 'ctx', ax...  36.2 us
    all_to_all x1, starting transfers between devices, body(): lax.all_to_all(partial_sums.reshape(ctx_count, tok_rows, 2 * head_dim), '...  12.6 us
    dynamic_update_slice x8, local copies, waits for them, and re-layouts, backward_step(): lax.dynamic_update_slice_in_dim(partial_sums, block_sums, key_start, 0)  4.17 us
    unnamed x8, local copies, waits for them, and re-layouts  3.82 us
    reshape x1, local copies, waits for them, and re-layouts, body(): partial_sums.reshape(ctx_count, tok_rows, 2 * head_dim)  2.89 us
  transfers between devices with their start and end apart: 2, of which 2 were waited for; matrix products, arithmetic and copies ran while one was open for 4% of the time, Pallas kernels for 0%

profile of v1, /device:TPU:13, one launch (start us, length us, event | category | flops | bytes accessed | tf_op | source)
XLA Modules:
  0.0 135.8 jit_solution(2724904065656250198)
XLA Ops:
  7.2 0.0 all-gather.2.cloned.1.call-start
  7.2 1.4 %pad_maximum_fusion.3 = bf16[128,256]{1,0:T(8,128)(2,1)} fusion(bf16[128,128]{1,0:T(8,128)(2,1)} %param.53, bf16[128,128]{1,0:T(8,128)(2,1)} %param.52), kind=kLoop, calls=%fused_computation.120 | loop fusion | flops 131072 | bytes 131072 | tf_op jit(solution)/shard_map/concatenate | solution.py:97
  8.6 0.0 all-gather.2.cloned.1.call-update
  8.7 0.7 fusion.61
  9.3 0.7 select_reduce_fusion.3
  10.1 1.0 multiply_convert_fusion.1
  11.1 0.2 copy.73
  11.3 0.2 copy.75
  11.5 1.1 copy.72
  12.6 0.2 copy.74
  12.8 0.1 pad_add_fusion
  12.8 36.2 %all-gather.2.cloned.1.call-done = bf16[2048,256]{1,0:T(8,128)(2,1)} async-done(((bf16[128,256]{1,0:T(8,128)(2,1)}), bf16[2048,256]{1,0:T(8,128)(2,1)}) %all-gather.2.cloned.1.call-update) | async-done | bytes 1048592 | tf_op jit(solution)/shard_map/all_gather | solution.py:97
  49.0 1.3 fusion.62
  50.3 3.9 %while.53 = (s32[]{:T(128)}, f32[128,6]{0,1:T(8,128)S(1)}, f32[128,6]{0,1:T(8,128)S(1)}, f32[128,6]{0,1:T(8,128)S(1)}, s32[]{:T(128)}, /*index=5*/s32[]{:T(128)}...) while((s32[]{:T(128)}, f32[128,6]{0,1:T(8,128)S(1)}, ...), condition=%wide.region_15.0_spmd.clone, body=%wide.region_1.15_spmd.clone.sunk | while | flops 205327120 | bytes 6221379 | solution.py:110
  50.4 1.7 %conditional.6 = ((f32[128,6]{0,1:T(8,128)S(1)}, f32[128,6]{0,1:T(8,128)S(1)}, f32[128,6]{0,1:T(8,128)S(1)})) conditional(s32[]{:T(128)} %clamp.18, (f32[128,6]{0,1:T(8,128)S(1)}, f32[128,6]{0,1:T(8,128)S(1)}, f32[128,6]{0,1:T(8,128)S(1)}) %tuple.203, (f32[128,6]{0,1:T(8,128)S(1)}, s32[]{:T(128)}, s32[]{:T(128)}, ...), branch_computations={%region_2.2_spmd, %region_3.6_spmd, %region_7.10_spmd, %region_11.... | conditional | flops 205327104 | bytes 5696036 | solution.py:61
  50.5 0.1 broadcast_compare_fusion.2
  50.6 0.5 select_reduce_fusion.2
  51.0 0.6 multiply_reduce_fusion
  51.6 0.5 fusion.20
  52.2 1.7 %conditional.6 = ((f32[128,6]{0,1:T(8,128)S(1)}, f32[128,6]{0,1:T(8,128)S(1)}, f32[128,6]{0,1:T(8,128)S(1)})) conditional(s32[]{:T(128)} %clamp.18, (f32[128,6]{0,1:T(8,128)S(1)}, f32[128,6]{0,1:T(8,128)S(1)}, f32[128,6]{0,1:T(8,128)S(1)}) %tuple.203, (f32[128,6]{0,1:T(8,128)S(1)}, s32[]{:T(128)}, s32[]{:T(128)}, ...), branch_computations={%region_2.2_spmd, %region_3.6_spmd, %region_7.10_spmd, %region_11.... | conditional | flops 205327104 | bytes 5696036 | solution.py:61
  52.3 0.1 broadcast_compare_fusion.2
  52.4 0.5 select_reduce_fusion.2
  52.9 0.6 multiply_reduce_fusion
  53.4 0.5 fusion.20
  54.3 1.5 %broadcast_in_dim.124.clone = f32[2048,256]{1,0:T(8,128)} broadcast(f32[]{:T(128)} %constant.488.clone.1), dimensions={} | broadcast | bytes 2097156 | tf_op jit(solution)/shard_map/broadcast_in_dim | solution.py:175
  55.8 8.7 %while.54 = (s32[]{:T(128)}, f32[128,6,128]{2,0,1:T(8,128)S(1)}, f32[2048,256]{1,0:T(8,128)}, s32[]{:T(128)}, s32[]{:T(128)}, /*index=5*/bf16[2048,128]{1,0:T(8,...) while((s32[]{:T(128)}, f32[128,6,128]{2,0,1:T(8,128)S(1)}, ...), condition=%wide.region_21.22_spmd.clone, body=%wide.region_16.21_spmd.clone.sunk | while | flops 506528256 | bytes 13381159 | solution.py:171
  55.8 2.1 %conditional.7 = (f32[128,6,128]{2,0,1:T(8,128)S(1)}, f32[512,256]{0,1:T(8,128)S(1)}) conditional(s32[]{:T(128)} %clamp.19, f32[128,6,128]{2,0,1:T(8,128)S(1)} %get-tuple-element.1423, (f32[128,6,128]{2,0,1:T(8,128)S(1)}, s32[]{:T(128)}, s32[]{:T(128)}, bf16[128,6,128]{0,2,1:T(8,128)(2,1)S(1)}, ...), branch_computations={%region_17.17_spmd, %region_18.18_spmd, %region_19.19_spmd, %regio... | conditional | flops 506528256 | bytes 10758676 | solution.py:61
  55.8 0.1 broadcast_compare_fusion.5
  56.0 0.5 exponential_select_fusion.3
  56.5 0.3 convolution_bitcast_fusion.4
  56.8 0.4 multiply_convert_fusion
  57.2 0.3 fusion.56
  57.5 0.4 fusion.55
  57.9 0.2 copy.91
  58.1 0.8 constant_dynamic-update-slice_fusion.2
  59.0 2.1 %conditional.7 = (f32[128,6,128]{2,0,1:T(8,128)S(1)}, f32[512,256]{0,1:T(8,128)S(1)}) conditional(s32[]{:T(128)} %clamp.19, f32[128,6,128]{2,0,1:T(8,128)S(1)} %get-tuple-element.1423, (f32[128,6,128]{2,0,1:T(8,128)S(1)}, s32[]{:T(128)}, s32[]{:T(128)}, bf16[128,6,128]{0,2,1:T(8,128)(2,1)S(1)}, ...), branch_computations={%region_17.17_spmd, %region_18.18_spmd, %region_19.19_spmd, %regio... | conditional | flops 506528256 | bytes 10758676 | solution.py:61
  59.0 0.1 broadcast_compare_fusion.5
  59.1 0.5 exponential_select_fusion.3
  59.7 0.3 convolution_bitcast_fusion.4
  59.9 0.4 multiply_convert_fusion
  60.4 0.3 fusion.56
  60.6 0.4 fusion.55
  61.1 0.2 copy.91
  61.3 0.9 constant_dynamic-update-slice_fusion.2
  62.1 0.1 conditional.7
  62.2 0.1 broadcast.400
  62.3 0.2 copy.91
  62.5 0.9 constant_dynamic-update-slice_fusion.2
  63.3 0.1 conditional.7
  63.4 0.1 broadcast.400
  63.4 0.2 copy.91
  63.6 0.9 constant_dynamic-update-slice_fusion.2
  64.5 0.0 copy-start
  64.5 2.9 %copy.78 = f32[16,128,256]{1,2,0:T(8,128)} copy(f32[16,128,256]{2,1,0:T(8,128)} %bitcast.88) | data formatting | bytes 4194304 | tf_op jit(solution)/shard_map/reshape | solution.py:179
  67.4 0.0 copy-done
  67.4 12.6 %all-to-all-start = ((f32[16,128,256]{1,2,0:T(8,128)}), f32[16,128,256]{1,2,0:T(8,128)S(1)}, u32[]{:S(2)}, u32[]{:S(2)}) async-start(f32[16,128,256]{1,2,0:T(8,128)} %copy.78), calls=%async_computation | async-start | bytes 4194304 | tf_op jit(solution)/shard_map/all_to_all | solution.py:178
  80.0 0.2 copy.76
  80.1 0.9 copy.80
  81.1 46.3 %all-to-all-done = f32[16,128,256]{1,2,0:T(8,128)S(1)} async-done(((f32[16,128,256]{1,2,0:T(8,128)}), f32[16,128,256]{1,2,0:T(8,128)S(1)}, u32[]{:S(2)}, u32[]{:S(2)}) %all-to-all-start) | async-done | bytes 2097184 | tf_op jit(solution)/shard_map/all_to_all | solution.py:178
  127.4 0.1 reduce_sum.73
  127.5 0.7 copy.82
  128.2 0.7 copy.81
  (45 shorter events, 0.5 us)
Async XLA Ops:
  7.2 41.9 %all-gather.2.cloned.1.call-start = ((), (), s32[]{:S(2)}) async-start(), calls=%async_computation.1 | async-start | bytes 1114112 | tf_op jit(solution)/shard_map/all_gather | solution.py:97
  64.5 2.9 %copy-start = (f32[128,6]{0,1:T(8,128)}, f32[128,6]{0,1:T(8,128)S(1)}, u32[]{:S(2)}) copy-start(f32[128,6]{0,1:T(8,128)S(1)} %get-tuple-element.1475) | copy-start | bytes 9220
  67.4 60.0 %all-to-all-start = ((f32[16,128,256]{1,2,0:T(8,128)}), f32[16,128,256]{1,2,0:T(8,128)S(1)}, u32[]{:S(2)}, u32[]{:S(2)}) async-start(f32[16,128,256]{1,2,0:T(8,128)} %copy.78), calls=%async_computation | async-start | bytes 4194304 | tf_op jit(solution)/shard_map/all_to_all | solution.py:178
Sparse Core Ops, SparseCore 0:
  10.7 38.2 all-gather.1
